TPU v7x, 128 devices: a whole 4x4x4 slice. The times are simulated.
128 devices in a mesh: img: 8 (over z_hi, y), cap: 16 (over x, z_lo, core).
Axes of the slice: x: 4, y: 4, z: 4 (z_hi: 2, z_lo: 2; z = z_hi * 2 + z_lo), core: 2. Of those that a mesh axis runs over, the one named last changes fastest.
Arguments:
- images: float32 [16384, 768], P('img'), may hold values from -100 to 100
- captions: float32 [16384, 768], P('cap', 'img'), may hold values from -8 to 8
- bank: float32 [16384, 768], P('img'), may hold values from -100 to 100
Outputs:
- expected: float32 [16384, 768], P('img')
All inputs are finite; a program needn't handle non-finite values.
Results may differ from a plain program's by a relative error of at most 0.0003.
Values sent between devices are 32-bit elements; how exact they have to be, the bound alone decides.
No kernel may reach another device: no remote copies, remote signals or barrier semaphores. Data moves between devices by JAX's collectives and lax.ppermute only.
A program may use at most 448 MiB of HBM per device.

v0:
```python
import jax
import jax.numpy as jnp
from jax import lax
from jax.sharding import PartitionSpec as P

exponent_divisor = 0.03


def similar(query_factor, target_factor):
    return exponent_divisor * lax.dot_general(
        query_factor,
        target_factor,
        (((1,), (1,)), ((), ())),
        precision=lax.Precision.HIGHEST,
        preferred_element_type=jnp.float32,
    )


def rescaled_affinity(weights, features):
    return jnp.dot(
        weights, features, precision=lax.Precision.HIGHEST, preferred_element_type=jnp.float32
    )


def local(images, captions, bank):
    features = lax.all_gather(captions, "img", axis=1, tiled=True)
    querybank_similarity = similar(bank, features)
    local_peak = jnp.max(querybank_similarity, axis=0)
    peak = lax.pmax(local_peak, "img")
    total = lax.psum(jnp.sum(jnp.exp(querybank_similarity - peak[None, :]), axis=0), "img")
    col_log = peak + jnp.log(total)
    logits = similar(images, features) - col_log[None, :]
    row_peak = jnp.max(logits, axis=1)
    top = lax.pmax(row_peak, "cap")
    weights = jnp.exp(logits - top[:, None])
    summed, row_total = lax.psum(
        (rescaled_affinity(weights, features), jnp.sum(weights, axis=1)), "cap"
    )
    result = summed / row_total[:, None]
    return result


def solution(mesh):
    return jax.shard_map(
        local,
        mesh=mesh,
        in_specs=(P("img", None), P("cap", "img"), P("img", None)),
        out_specs=P("img", None),
        check_vma=False,
    )
```

profile of v0, /device:TPU:5, one launch (start us, length us, event | category | flops | bytes accessed | tf_op | source)
XLA Modules:
  0.0 408.6 jit_solution(2662504765495585626)
XLA Ops:
  6.5 0.0 all-gather.2.cloned.1.call-start
  6.5 0.7 all-gather.2.cloned.1.call-update
  7.3 0.0 all-reduce.2.cloned.1.call-start
  7.3 67.5 %all-gather.2.cloned.1.call-done = f32[1024,768]{0,1:T(8,128)} async-done(((f32[1024,96]{0,1:T(8,128)}), f32[1024,768]{0,1:T(8,128)}) %all-gather.2.cloned.1.call-update) | async-done | bytes 3145744 | tf_op jit(solution)/shard_map/all_gather | solution.py:26
  74.8 25.2 %multiply_reduce_fusion = (f32[1024]{0:T(1024)S(1)}, f32[2048,1024]{0,1:T(8,128)}) fusion(f32[2048,768]{1,0:T(8,128)} %param.5, f32[1024,768]{0,1:T(8,128)} %all-gather.2.cloned.1.call-done), kind=kOutput, calls=%fused_computation.3 | convolution fusion | flops 19331547136 | bytes 17829888 | tf_op jit(solution)/shard_map/dot_general | solution.py:10
  100.0 0.0 copy-start
  100.0 16.3 %pmax.14 = f32[1024]{0:T(1024)S(1)} all-reduce(f32[1024]{0:T(1024)S(1)} %get-tuple-element.5), channel_id=1, replica_groups=mesh['img'=8,'cap'=16] {'img'}, use_global_device_ids=true, to_apply=%region_1.0 | all-reduce | flops 1024 | bytes 8192 | tf_op jit(solution)/shard_map/pmax | solution.py:29
  116.3 4.4 %exponential_reduce_fusion = f32[1024]{0:T(1024)S(1)} fusion(f32[2048,1024]{0,1:T(8,128)} %get-tuple-element.6, f32[1024]{0:T(1024)S(1)} %pmax.14), kind=kLoop, calls=%fused_computation.1 | loop fusion | flops 6290432 | bytes 8396800 | tf_op jit(solution)/shard_map/reduce_sum | solution.py:30
  120.7 16.5 %psum.21 = f32[1024]{0:T(1024)S(1)} all-reduce(f32[1024]{0:T(1024)S(1)} %exponential_reduce_fusion), channel_id=1, replica_groups=mesh['img'=8,'cap'=16] {'img'}, use_global_device_ids=true, to_apply=%region_3.0 | all-reduce | flops 1024 | bytes 8192 | tf_op jit(solution)/shard_map/psum | solution.py:30
  137.2 0.0 copy-done
  137.2 25.1 %fusion = (f32[2048]{0:T(1024)S(1)}, f32[2048,1024]{0,1:T(8,128)}) fusion(f32[1024]{0:T(1024)S(1)} %log_add_fusion, f32[2048,768]{1,0:T(8,128)} %param.3, f32[1024,768]{0,1:T(8,128)S(1)} %copy-done), kind=kOutput, calls=%fused_computation.4 | convolution fusion | flops 19333642240 | bytes 17838080 | tf_op jit(solution)/shard_map/dot_general | solution.py:10
  162.4 30.7 %pmax.15 = f32[2048]{0:T(1024)S(1)} all-reduce(f32[2048]{0:T(1024)S(1)} %get-tuple-element.7), channel_id=1, replica_groups=mesh['img'=8,'cap'=16] {'cap'}, use_global_device_ids=true, to_apply=%region_5.0 | all-reduce | flops 2048 | bytes 16384 | tf_op jit(solution)/shard_map/pmax | solution.py:34
  193.1 44.3 %fusion.2 = f32[2048,768]{1,0:T(8,128)} fusion(f32[1024,768]{0,1:T(8,128)S(1)} %copy-done, f32[2048,1024]{0,1:T(8,128)} %get-tuple-element.8, f32[2048]{0:T(1024)S(1)} %pmax.15, f32[1024]{0:T(1024)S(1)} %log_add_fusion), kind=kOutput, calls=%fused_computation.6 | convolution fusion | flops 19333644288 | bytes 17838080 | tf_op jit(solution)/shard_map/dot_general | solution.py:20
  237.5 0.0 all-reduce.2.cloned.1.call-update
  237.5 4.5 %fusion.1 = f32[2048]{0:T(1024)S(1)} fusion(f32[2048,1024]{0,1:T(8,128)} %get-tuple-element.8, f32[2048]{0:T(1024)S(1)} %pmax.15, f32[1024]{0:T(1024)S(1)} %log_add_fusion), kind=kLoop, calls=%fused_computation.5 | loop fusion | flops 8386560 | bytes 8409088 | tf_op jit(solution)/shard_map/reduce_sum | solution.py:37
  242.0 23.2 %psum.23 = f32[2048]{0:T(1024)S(1)} all-reduce(f32[2048]{0:T(1024)S(1)} %fusion.1), channel_id=1, replica_groups=mesh['img'=8,'cap'=16] {'cap'}, use_global_device_ids=true, to_apply=%region_8.0 | all-reduce | flops 2048 | bytes 16384 | tf_op jit(solution)/shard_map/psum | solution.py:36
  265.2 130.2 %all-reduce.2.cloned.1.call-done = f32[2048,768]{1,0:T(8,128)} async-done(((f32[2048,768]{1,0:T(8,128)}), f32[2048,768]{1,0:T(8,128)}) %all-reduce.2.cloned.1.call-update) | async-done | bytes 6291472 | tf_op jit(solution)/shard_map/psum | solution.py:36
  395.4 6.0 %broadcast_divide_fusion = f32[2048,768]{1,0:T(8,128)} fusion(f32[2048,768]{1,0:T(8,128)} %all-reduce.2.cloned.1.call-done, f32[2048]{0:T(1024)S(1)} %psum.23), kind=kLoop, calls=%fused_computation.10 | loop fusion | flops 1572864 | bytes 12591104 | tf_op jit(solution)/shard_map/div | solution.py:39
  (1 shorter events, 0.0 us)
Async XLA Ops:
  6.5 68.3 %all-gather.2.cloned.1.call-start = ((), (), s32[]{:S(2)}) async-start(), calls=%async_computation | async-start | bytes 3538944 | tf_op jit(solution)/shard_map/all_gather | solution.py:26
  7.3 388.2 %all-reduce.2.cloned.1.call-start = ((), (), s32[]{:S(2)}) async-start(), calls=%async_computation.1 | async-start | bytes 12582912 | tf_op jit(solution)/shard_map/psum | solution.py:36
  100.0 37.2 %copy-start = (f32[1024,768]{0,1:T(8,128)S(1)}, f32[1024,768]{0,1:T(8,128)}, u32[]{:S(2)}) copy-start(f32[1024,768]{0,1:T(8,128)} %all-gather.2.cloned.1.call-done) | copy-start | bytes 9437188
Sparse Core Ops, SparseCore 0:
  9.7 65.0 all-gather.1
  237.6 157.7 all-reduce.1
where the time goes:
time: 417 us; the launch traced here: 409 us
  waiting for transfers between devices  198 us (47%)
  matrix products  94.7 us (23%)
  blocking collectives  86.8 us (21%)
  other arithmetic  14.9 us (4%)
  between operations  13.8 us (3%)
    psum x1, waiting for transfers between devices, local(): lax.psum((rescaled_affinity(weights, features), jnp.sum(weights, axis=1))...  130 us
    all_gather x1, waiting for transfers between devices, local(): features = lax.all_gather(captions, 'img', axis=1, tiled=True)  67.5 us
    dot_general x2, matrix products, similar(): lax.dot_general(query_factor, target_factor, (((1,), (1,)), ((), ())), pr...  50.4 us
    dot_general x1, matrix products, rescaled_affinity(): jnp.dot(weights, features, precision=lax.Precision.HIGHEST, preferred_ele...  44.3 us
    pmax x1, blocking collectives, local(): top = lax.pmax(row_peak, 'cap')  30.7 us
    psum x1, blocking collectives, local(): lax.psum((rescaled_affinity(weights, features), jnp.sum(weights, axis=1))...  23.2 us
    psum x1, blocking collectives, local(): lax.psum(jnp.sum(jnp.exp(querybank_similarity - peak[None, :]), axis=0),...  16.5 us
    pmax x1, blocking collectives, local(): peak = lax.pmax(local_peak, 'img')  16.3 us
  transfers between devices with their start and end apart: 2, of which 2 were waited for; matrix products, arithmetic and copies ran while one was open for 1% of the time, Pallas kernels for 0%

commit v1 on v0

--- a/solution.py
+++ b/solution.py
@@ -27,7 +27,10 @@
     querybank_similarity = similar(bank, features)
     local_peak = jnp.max(querybank_similarity, axis=0)
     peak = lax.pmax(local_peak, "img")
-    total = lax.psum(jnp.sum(jnp.exp(querybank_similarity - peak[None, :]), axis=0), "img")
+    total = jnp.sum(
+        lax.all_gather(jnp.sum(jnp.exp(querybank_similarity - peak[None, :]), axis=0), "img"),
+        axis=0,
+    )
     col_log = peak + jnp.log(total)
     logits = similar(images, features) - col_log[None, :]
     row_peak = jnp.max(logits, axis=1)

time: 417 us -> 430 us (1.031)
  blocking collectives: 86.8 us -> 103 us
    all_gather x0 -> x1, blocking collectives: none -> 27.7 us  [local(): lax.all_gather(jnp.sum(jnp.exp(querybank_similarity - peak[None, :]), axi...]
    psum x1 -> x0, blocking collectives: 16.5 us -> none  [local(): lax.psum(jnp.sum(jnp.exp(querybank_similarity - peak[None, :]), axis=0),...]
where the time goes in v1:
time: 430 us; the launch traced here: 422 us
  waiting for transfers between devices  196 us (46%)
  blocking collectives  103 us (24%)
  matrix products  94.7 us (22%)
  other arithmetic  14.9 us (3%)
  between operations  13.8 us (3%)
    psum x1, waiting for transfers between devices, local(): lax.psum((rescaled_affinity(weights, features), jnp.sum(weights, axis=1))...  128 us
    all_gather x1, waiting for transfers between devices, local(): features = lax.all_gather(captions, 'img', axis=1, tiled=True)  67.5 us
    dot_general x2, matrix products, similar(): lax.dot_general(query_factor, target_factor, (((1,), (1,)), ((), ())), pr...  50.3 us
    dot_general x1, matrix products, rescaled_affinity(): jnp.dot(weights, features, precision=lax.Precision.HIGHEST, preferred_ele...  44.3 us
    pmax x1, blocking collectives, local(): top = lax.pmax(row_peak, 'cap')  34.5 us
    all_gather x1, blocking collectives, local(): lax.all_gather(jnp.sum(jnp.exp(querybank_similarity - peak[None, :]), axi...  27.7 us
    psum x1, blocking collectives, local(): lax.psum((rescaled_affinity(weights, features), jnp.sum(weights, axis=1))...  24 us
    pmax x1, blocking collectives, local(): peak = lax.pmax(local_peak, 'img')  16.3 us
  transfers between devices with their start and end apart: 2, of which 2 were waited for; matrix products, arithmetic and copies ran while one was open for 1% of the time, Pallas kernels for 0%

profile of v1, /device:TPU:5, one launch (start us, length us, event | category | flops | bytes accessed | tf_op | source)
XLA Modules:
  0.0 421.9 jit_solution(16876786846377444876)
XLA Ops:
  6.5 0.0 all-gather.3.cloned.1.call-start
  6.5 0.7 all-gather.3.cloned.1.call-update
  7.3 0.0 all-reduce.2.cloned.1.call-start
  7.3 67.5 %all-gather.3.cloned.1.call-done = f32[1024,768]{0,1:T(8,128)} async-done(((f32[1024,96]{0,1:T(8,128)}), f32[1024,768]{0,1:T(8,128)}) %all-gather.3.cloned.1.call-update) | async-done | bytes 3145744 | tf_op jit(solution)/shard_map/all_gather | solution.py:26
  74.8 25.2 %multiply_reduce_fusion = (f32[1024]{0:T(1024)S(1)}, f32[2048,1024]{0,1:T(8,128)}) fusion(f32[2048,768]{1,0:T(8,128)} %param.5, f32[1024,768]{0,1:T(8,128)} %all-gather.3.cloned.1.call-done), kind=kOutput, calls=%fused_computation.3 | convolution fusion | flops 19331547136 | bytes 17829888 | tf_op jit(solution)/shard_map/dot_general | solution.py:10
  100.0 0.0 copy-start
  100.0 16.3 %pmax.14 = f32[1024]{0:T(1024)S(1)} all-reduce(f32[1024]{0:T(1024)S(1)} %get-tuple-element.5), channel_id=1, replica_groups=mesh['img'=8,'cap'=16] {'img'}, use_global_device_ids=true, to_apply=%region_1.0 | all-reduce | flops 1024 | bytes 8192 | tf_op jit(solution)/shard_map/pmax | solution.py:29
  116.3 4.4 %exponential_reduce_fusion = f32[1024]{0:T(1024)S(1)} fusion(f32[2048,1024]{0,1:T(8,128)} %get-tuple-element.6, f32[1024]{0:T(1024)S(1)} %pmax.14), kind=kLoop, calls=%fused_computation.1 | loop fusion | flops 6290432 | bytes 8396800 | tf_op jit(solution)/shard_map/reduce_sum | solution.py:31
  120.7 27.7 %all-gather = f32[8192]{0:T(1024)S(1)} all-gather(f32[1024]{0:T(1024)S(1)} %exponential_reduce_fusion), channel_id=2, replica_groups=mesh['img'=8,'cap'=16] {'img'}, dimensions={0}, use_global_device_ids=true | all-gather | bytes 36864 | tf_op jit(solution)/shard_map/all_gather | solution.py:31
  148.5 0.0 copy-done
  148.5 25.1 %fusion = (f32[2048]{0:T(1024)S(1)}, f32[2048,1024]{0,1:T(8,128)}) fusion(f32[1024]{0:T(1024)S(1)} %log_add_fusion, f32[2048,768]{1,0:T(8,128)} %param.3, f32[1024,768]{0,1:T(8,128)S(1)} %copy-done), kind=kOutput, calls=%fused_computation.4 | convolution fusion | flops 19333642240 | bytes 17838080 | tf_op jit(solution)/shard_map/dot_general | solution.py:10
  173.6 34.5 %pmax.15 = f32[2048]{0:T(1024)S(1)} all-reduce(f32[2048]{0:T(1024)S(1)} %get-tuple-element.7), channel_id=1, replica_groups=mesh['img'=8,'cap'=16] {'cap'}, use_global_device_ids=true, to_apply=%region_5.0 | all-reduce | flops 2048 | bytes 16384 | tf_op jit(solution)/shard_map/pmax | solution.py:37
  208.1 44.3 %fusion.2 = f32[2048,768]{1,0:T(8,128)} fusion(f32[1024,768]{0,1:T(8,128)S(1)} %copy-done, f32[2048,1024]{0,1:T(8,128)} %get-tuple-element.8, f32[2048]{0:T(1024)S(1)} %pmax.15, f32[1024]{0:T(1024)S(1)} %log_add_fusion), kind=kOutput, calls=%fused_computation.6 | convolution fusion | flops 19333644288 | bytes 17838080 | tf_op jit(solution)/shard_map/dot_general | solution.py:20
  252.4 0.0 all-reduce.2.cloned.1.call-update
  252.4 4.5 %fusion.1 = f32[2048]{0:T(1024)S(1)} fusion(f32[2048,1024]{0,1:T(8,128)} %get-tuple-element.8, f32[2048]{0:T(1024)S(1)} %pmax.15, f32[1024]{0:T(1024)S(1)} %log_add_fusion), kind=kLoop, calls=%fused_computation.5 | loop fusion | flops 8386560 | bytes 8409088 | tf_op jit(solution)/shard_map/reduce_sum | solution.py:40
  257.0 24.0 %psum.15 = f32[2048]{0:T(1024)S(1)} all-reduce(f32[2048]{0:T(1024)S(1)} %fusion.1), channel_id=1, replica_groups=mesh['img'=8,'cap'=16] {'cap'}, use_global_device_ids=true, to_apply=%region_8.0 | all-reduce | flops 2048 | bytes 16384 | tf_op jit(solution)/shard_map/psum | solution.py:39
  281.0 127.7 %all-reduce.2.cloned.1.call-done = f32[2048,768]{1,0:T(8,128)} async-done(((f32[2048,768]{1,0:T(8,128)}), f32[2048,768]{1,0:T(8,128)}) %all-reduce.2.cloned.1.call-update) | async-done | bytes 6291472 | tf_op jit(solution)/shard_map/psum | solution.py:39
  408.7 6.0 %broadcast_divide_fusion = f32[2048,768]{1,0:T(8,128)} fusion(f32[2048,768]{1,0:T(8,128)} %all-reduce.2.cloned.1.call-done, f32[2048]{0:T(1024)S(1)} %psum.15), kind=kLoop, calls=%fused_computation.10 | loop fusion | flops 1572864 | bytes 12591104 | tf_op jit(solution)/shard_map/div | solution.py:42
  (3 shorter events, 0.0 us)
Async XLA Ops:
  6.5 68.3 %all-gather.3.cloned.1.call-start = ((), (), s32[]{:S(2)}) async-start(), calls=%async_computation | async-start | bytes 3538944 | tf_op jit(solution)/shard_map/all_gather | solution.py:26
  7.3 401.5 %all-reduce.2.cloned.1.call-start = ((), (), s32[]{:S(2)}) async-start(), calls=%async_computation.1 | async-start | bytes 12582912 | tf_op jit(solution)/shard_map/psum | solution.py:39
  100.0 48.4 %copy-start = (f32[1024,768]{0,1:T(8,128)S(1)}, f32[1024,768]{0,1:T(8,128)}, u32[]{:S(2)}) copy-start(f32[1024,768]{0,1:T(8,128)} %all-gather.3.cloned.1.call-done) | copy-start | bytes 9437188
Sparse Core Ops, SparseCore 0:
  9.7 65.0 all-gather.2
  252.6 156.1 all-reduce.1
